TPU v7x, 256 devices: a whole 4x4x8 slice. The times are simulated.
256 devices in a mesh: gx: 32 (over x, y, core), gy: 8 (over z).
Axes of the slice: x: 4, y: 4, z: 8, core: 2. Of those that a mesh axis runs over, the one named last changes fastest.
Arguments:
- orbitals: float32 [64, 128, 64, 128], P(None, 'gx', 'gy'), may hold values from -60 to 60, as said below
- potential: float32 [128, 64, 128], P('gx', 'gy'), may hold values from 0.2 to 2
Outputs:
- basis: float32 [64, 128, 64, 128], P(None, 'gx', 'gy')
- factor: float32 [64, 64], replicated
Inputs may be any that keep to these rules, and one draw needn't show every extreme that they name: `orbitals`: Real-valued entries.
All inputs are finite; a program needn't handle non-finite values.
Results may differ from a plain program's by a relative error of at most 0.00011.
Values sent between devices are 32-bit elements; how exact they have to be, the bound alone decides.
No kernel may reach another device: no remote copies, remote signals or barrier semaphores. Data moves between devices by JAX's collectives and lax.ppermute only.
A program may use at most 64 MiB of HBM per device.

v0:
```python
import jax
import jax.numpy as jnp
from jax import lax
from jax.sharding import PartitionSpec as P


def extended(cells, sides, width):
    for axis, dim in sides:
        count = lax.axis_size(axis)
        head = lax.slice_in_dim(cells, 0, width, axis=dim)
        tail = lax.slice_in_dim(cells, cells.shape[dim] - width, cells.shape[dim], axis=dim)
        cells = jnp.concatenate(
            [
                lax.ppermute(tail, axis, [(i, (i + 1) % count) for i in range(count)]),
                cells,
                lax.ppermute(head, axis, [((i + 1) % count, i) for i in range(count)]),
            ],
            axis=dim,
        )
    return cells


def apply_ham(padded, pot):
    core = padded[:, 2:-2, 2:-2]
    total = -7.5 * core
    total = total + 4.0 / 3.0 * (padded[:, 3:-1, 2:-2] + padded[:, 1:-3, 2:-2])
    total = total - 1.0 / 12.0 * (padded[:, 4:, 2:-2] + padded[:, :-4, 2:-2])
    total = total + 4.0 / 3.0 * (padded[:, 2:-2, 3:-1] + padded[:, 2:-2, 1:-3])
    total = total - 1.0 / 12.0 * (padded[:, 2:-2, 4:] + padded[:, 2:-2, :-4])
    total = total + 4.0 / 3.0 * (jnp.roll(core, 1, 3) + jnp.roll(core, -1, 3))
    total = total - 1.0 / 12.0 * (jnp.roll(core, 2, 3) + jnp.roll(core, -2, 3))
    return -0.5 * total + pot[None] * core


def with_faces(field):
    return extended(field, (("gx", 1), ("gy", 2)), 2)


def upper_factor(gram):
    order = gram.shape[0]
    index = jnp.arange(order)

    def column_step(col, lower):
        row_now = lax.dynamic_slice_in_dim(lower, col, 1, 0)[0]
        target = lax.dynamic_slice_in_dim(gram, col, 1, 1)[:, 0]
        column = target - jnp.dot(
            lower, row_now, precision=lax.Precision.HIGHEST, preferred_element_type=jnp.float32
        )
        pivot = jnp.sqrt(jnp.sum(jnp.where(index == col, column, 0.0)))
        values = jnp.where(index == col, pivot, column / pivot)
        values = jnp.where(index >= col, values, 0.0)
        return jnp.where(index[None, :] == col, values[:, None], lower)

    lower = lax.fori_loop(0, order, column_step, jnp.zeros_like(gram))
    return lower.T


def upper_inverse(upper):
    order = upper.shape[0]
    index = jnp.arange(order)

    def row_step(step, inverse):
        row = order - 1 - step
        upper_row = lax.dynamic_slice_in_dim(upper, row, 1, 0)[0]
        pivot = jnp.sum(jnp.where(index == row, upper_row, 0.0))
        rest = jnp.dot(
            upper_row, inverse, precision=lax.Precision.HIGHEST, preferred_element_type=jnp.float32
        )
        unit = jnp.where(index == row, 1.0, 0.0).astype(jnp.float32)
        new_row = (unit - rest) / pivot
        return jnp.where(index[:, None] == row, new_row[None, :], inverse)

    return lax.fori_loop(0, order, row_step, jnp.zeros_like(upper))


def shards(orbitals, potential):
    first = (apply_ham(with_faces(orbitals), potential) - 5.5 * orbitals) / 4.5
    applied = apply_ham(with_faces(first), potential)
    filtered = 2.0 * (applied - 5.5 * first) / 4.5 - orbitals
    width = filtered.shape[0]
    flat = filtered.reshape(width, -1)
    cells = flat.shape[1] * lax.axis_size("gx") * lax.axis_size("gy")
    local_gram = (
        jnp.dot(flat, flat.T, precision=lax.Precision.HIGHEST, preferred_element_type=jnp.float32)
        / cells
    )
    factor = upper_factor(lax.psum(local_gram, ("gx", "gy")))
    inverse = upper_inverse(factor)
    solved = jnp.dot(
        inverse.T, flat, precision=lax.Precision.HIGHEST, preferred_element_type=jnp.float32
    )
    basis = (solved * jnp.sqrt(jnp.float32(cells))).reshape(filtered.shape)
    return (basis, factor)


def solution(mesh):
    return jax.shard_map(
        shards,
        mesh=mesh,
        in_specs=(P(None, "gx", "gy", None), P("gx", "gy", None)),
        out_specs=(P(None, "gx", "gy", None), P()),
        check_vma=False,
    )
```

profile of v0, /device:TPU:1, one launch (start us, length us, event | category | flops | bytes accessed | tf_op | source)
XLA Modules:
  0.0 353.4 jit_solution(158170441676691293)
XLA Ops:
  0.6 2.4 fusion.60
  3.0 3.2 collective-permute-start
  8.3 4.5 %collective-permute-done = f32[64,2,8,128]{3,2,1,0:T(8,128)S(1)} collective-permute-done((f32[64,2,8,128]{3,2,1,0:T(8,128)}, f32[64,2,8,128]{3,2,1,0:T(8,128)S(1)}, u32[]{:S(2)}, u32[]{:S(2)}) %collective-permute-start) | collective-permute-done | bytes 524320 | tf_op jit(solution)/shard_map/ppermute | solution.py:16
  13.7 5.7 %collective-permute-start.2 = (f32[64,8,2,128]{3,1,2,0:T(8,128)S(1)}, f32[64,8,2,128]{3,1,2,0:T(8,128)S(1)}, u32[]{:S(2)}, u32[]{:S(2)}) collective-permute-start(f32[64,8,2,128]{3,1,2,0:T(8,128)S(1)} %get-tuple-element.266), channel_id=1, source_target_pairs={{1,0},{2,1},{3,2},{4,3},{5,4},{6,5},{7,6},{0,7},{9,8},{10,9},{11,1... | collective-permute-start | bytes 1572872 | tf_op jit(solution)/shard_map/ppermute | solution.py:16
  20.6 4.8 %collective-permute-done.2 = f32[64,8,2,128]{3,1,2,0:T(8,128)S(1)} collective-permute-done((f32[64,8,2,128]{3,1,2,0:T(8,128)S(1)}, f32[64,8,2,128]{3,1,2,0:T(8,128)S(1)}, u32[]{:S(2)}, u32[]{:S(2)}) %collective-permute-start.2) | collective-permute-done | bytes 524320 | tf_op jit(solution)/shard_map/ppermute | solution.py:16
  25.4 3.1 collective-permute-done.3
  28.6 7.3 %broadcast_multiply_fusion = (f32[64,4,8,128]{3,1,2,0:T(4,128)S(1)}, f32[64,4,8,128]{3,1,2,0:T(4,128)S(1)}) fusion(f32[64,4,8,128]{3,1,2,0:T(4,128)S(1)} %copy.55, f32[4,8,128]{2,0,1:T(4,128)S(1)} %copy.71, f32[64,4,8,2]{3,1,2,0:T(4,128)S(1)} %get-tuple-element.285, f32[64,4,8,126]{3,1,2,0:T(4,128)S(1)} %get-tuple-element.287, ...), kind=kLoop, calls=%fused_computation.105 | loop fusion | flops 11796480 | bytes 9453568 | tf_op jit(solution)/shard_map/div | solution.py:77
  36.4 9.8 %collective-permute-start.4 = (f32[64,2,8,128]{3,2,1,0:T(8,128)S(1)}, f32[64,2,8,128]{3,2,1,0:T(8,128)S(1)}, u32[]{:S(2)}, u32[]{:S(2)}) collective-permute-start(f32[64,2,8,128]{3,2,1,0:T(8,128)S(1)} %copy.74), channel_id=1, source_target_pairs={{8,0},{16,8},{24,16},{32,24},{40,32},{48,40},{56,48},{64,56},{72,6... | collective-permute-start | bytes 1572872 | tf_op jit(solution)/shard_map/ppermute | solution.py:16
  47.7 3.3 collective-permute-done.4
  51.3 1.3 collective-permute-done.5
  53.3 1.5 collective-permute-start.7
  56.0 5.3 %collective-permute-done.6 = f32[64,8,2,128]{3,1,2,0:T(8,128)S(1)} collective-permute-done((f32[64,8,2,128]{3,1,2,0:T(8,128)S(1)}, f32[64,8,2,128]{3,1,2,0:T(8,128)S(1)}, u32[]{:S(2)}, u32[]{:S(2)}) %collective-permute-start.6) | collective-permute-done | bytes 524320 | tf_op jit(solution)/shard_map/ppermute | solution.py:16
  61.3 1.3 collective-permute-done.7
  62.6 7.5 %multiply_subtract_fusion = f32[64,4,8,128]{3,1,2,0:T(4,128)S(1)} fusion(f32[64,4,8,128]{3,1,2,0:T(4,128)S(1)} %get-tuple-element.261, f32[64,4,8,2]{3,1,2,0:T(4,128)S(1)} %get-tuple-element.275, f32[64,4,8,126]{3,1,2,0:T(4,128)S(1)} %get-tuple-element.277, f32[64,4,8,126]{3,1,2,0:T(4,128)S(1)} %get-tuple-element.276, ...), kind=kLoop, calls=%fused_computation.97 | loop fusion | flops 12058624 | bytes 10502144 | tf_op jit(solution)/shard_map/sub | solution.py:79
  70.1 2.1 fusion.17
  72.2 81.9 %psum.7 = f32[64,64]{1,0:T(8,128)S(1)} all-reduce(f32[64,64]{1,0:T(8,128)S(1)} %fusion.17), channel_id=1, replica_groups=mesh['gx'=32,'gy'=8] {'gx','gy'}, use_global_device_ids=true, to_apply=%region_0.1 | all-reduce | flops 4096 | bytes 32768 | tf_op jit(solution)/shard_map/psum | solution.py:87
  154.2 101.3 %while.32 = (s32[]{:T(128)}, f32[64,64]{1,0:T(8,128)S(1)}, f32[64,64]{0,1:T(8,128)S(1)}, s32[]{:T(128)}, s32[]{:T(128)}) while((s32[]{:T(128)}, f32[64,64]{1,0:T(8,128)S(1)}, f32[64,64]{0,1:T(8,128)S(1)}, s32[]{:T(128)}, s32[]{:T(128)}) %tuple.94), condition=%wide.region_3.4_spmd.clone.clone, body=%wide.region_1.3_spmd.clone.clone.sunk | while | flops 62082 | bytes 102112 | solution.py:54
  255.6 95.1 %while.31 = (s32[]{:T(128)}, f32[64,64]{1,0:T(8,128)S(1)}, f32[64,64]{1,0:T(8,128)S(1)}, s32[]{:T(128)}, s32[]{:T(128)}, /*index=5*/s32[]{:T(128)}, s32[]{:T(128)}) while((s32[]{:T(128)}, f32[64,64]{1,0:T(8,128)S(1)}, f32[64,64]{1,0:T(8,128)S(1)}, s32[]{:T(128)}, s32[]{:T(128)}, /*index=5*/s32[]{:T(128)}, s32[]{:T(128)}) %tuple.100), condition=%wide.region_6.7_spmd.clone, body=%wide.region_4.6_spmd.clone.sunk | while | flops 61958 | bytes 67106 | solution.py:73
  256.2 0.8 fusion.75
  257.7 0.8 fusion.75
  259.1 0.8 fusion.75
  262.1 0.8 fusion.75
  263.6 0.8 fusion.75
  265.1 0.8 fusion.75
  266.6 0.8 fusion.75
  268.1 0.8 fusion.75
  271.0 0.8 fusion.75
  272.5 0.8 fusion.75
  274.0 0.8 fusion.75
  275.5 0.8 fusion.75
  350.6 1.6 fusion.16
  352.2 1.2 copy.89
  (601 shorter events, 149.5 us)
Async XLA Ops:
  0.6 5.6 %copy-start = (f32[64,4,8,128]{3,2,1,0:T(8,128)S(1)}, f32[64,4,8,128]{3,2,1,0:T(8,128)}, u32[]{:S(2)}) copy-start(f32[64,4,8,128]{3,2,1,0:T(8,128)} %param.6) | copy-start | bytes 3145732
  3.0 9.8 %collective-permute-start = (f32[64,2,8,128]{3,2,1,0:T(8,128)}, f32[64,2,8,128]{3,2,1,0:T(8,128)S(1)}, u32[]{:S(2)}, u32[]{:S(2)}) collective-permute-start(f32[64,2,8,128]{3,2,1,0:T(8,128)} %get-tuple-element.279), channel_id=1, source_target_pairs={{8,0},{16,8},{24,16},{32,24},{40,32},{48,40},{56,48},{64,56},{72,6... | collective-permute-start | bytes 1572872 | tf_op jit(solution)/shard_map/ppermute | solution.py:16
  6.2 0.7 copy-start.1
  6.2 6.8 %collective-permute-start.1 = (f32[64,2,8,128]{3,2,1,0:T(8,128)}, f32[64,2,8,128]{3,2,1,0:T(8,128)S(1)}, u32[]{:S(2)}, u32[]{:S(2)}) collective-permute-start(f32[64,2,8,128]{3,2,1,0:T(8,128)} %get-tuple-element.278), channel_id=1, source_target_pairs={{0,8},{8,16},{16,24},{24,32},{32,40},{40,48},{48,56},{56,64},{64,7... | collective-permute-start | bytes 1572872 | tf_op jit(solution)/shard_map/ppermute | solution.py:14
  13.7 11.8 %collective-permute-start.2 = (f32[64,8,2,128]{3,1,2,0:T(8,128)S(1)}, f32[64,8,2,128]{3,1,2,0:T(8,128)S(1)}, u32[]{:S(2)}, u32[]{:S(2)}) collective-permute-start(f32[64,8,2,128]{3,1,2,0:T(8,128)S(1)} %get-tuple-element.266), channel_id=1, source_target_pairs={{1,0},{2,1},{3,2},{4,3},{5,4},{6,5},{7,6},{0,7},{9,8},{10,9},{11,1... | collective-permute-start | bytes 1572872 | tf_op jit(solution)/shard_map/ppermute | solution.py:16
  19.3 9.2 %collective-permute-start.3 = (f32[64,8,2,128]{3,1,2,0:T(8,128)S(1)}, f32[64,8,2,128]{3,1,2,0:T(8,128)S(1)}, u32[]{:S(2)}, u32[]{:S(2)}) collective-permute-start(f32[64,8,2,128]{3,1,2,0:T(8,128)S(1)} %get-tuple-element.267), channel_id=1, source_target_pairs={{0,1},{1,2},{2,3},{3,4},{4,5},{5,6},{6,7},{7,0},{8,9},{9,10},{10,1... | collective-permute-start | bytes 1572872 | tf_op jit(solution)/shard_map/ppermute | solution.py:14
  36.4 14.6 %collective-permute-start.4 = (f32[64,2,8,128]{3,2,1,0:T(8,128)S(1)}, f32[64,2,8,128]{3,2,1,0:T(8,128)S(1)}, u32[]{:S(2)}, u32[]{:S(2)}) collective-permute-start(f32[64,2,8,128]{3,2,1,0:T(8,128)S(1)} %copy.74), channel_id=1, source_target_pairs={{8,0},{16,8},{24,16},{32,24},{40,32},{48,40},{56,48},{64,56},{72,6... | collective-permute-start | bytes 1572872 | tf_op jit(solution)/shard_map/ppermute | solution.py:16
  46.2 6.4 %collective-permute-start.5 = (f32[64,2,8,128]{3,2,1,0:T(8,128)S(1)}, f32[64,2,8,128]{3,2,1,0:T(8,128)S(1)}, u32[]{:S(2)}, u32[]{:S(2)}) collective-permute-start(f32[64,2,8,128]{3,2,1,0:T(8,128)S(1)} %copy.76), channel_id=1, source_target_pairs={{0,8},{8,16},{16,24},{24,32},{32,40},{40,48},{48,56},{56,64},{64,7... | collective-permute-start | bytes 1572872 | tf_op jit(solution)/shard_map/ppermute | solution.py:14
  53.2 8.1 %collective-permute-start.6 = (f32[64,8,2,128]{3,1,2,0:T(8,128)S(1)}, f32[64,8,2,128]{3,1,2,0:T(8,128)S(1)}, u32[]{:S(2)}, u32[]{:S(2)}) collective-permute-start(f32[64,8,2,128]{3,1,2,0:T(8,128)S(1)} %get-tuple-element.264), channel_id=1, source_target_pairs={{1,0},{2,1},{3,2},{4,3},{5,4},{6,5},{7,6},{0,7},{9,8},{10,9},{11,1... | collective-permute-start | bytes 1572872 | tf_op jit(solution)/shard_map/ppermute | solution.py:16
  53.3 9.3 %collective-permute-start.7 = (f32[64,8,2,128]{3,1,2,0:T(8,128)S(1)}, f32[64,8,2,128]{3,1,2,0:T(8,128)S(1)}, u32[]{:S(2)}, u32[]{:S(2)}) collective-permute-start(f32[64,8,2,128]{3,1,2,0:T(8,128)S(1)} %get-tuple-element.265), channel_id=1, source_target_pairs={{0,1},{1,2},{2,3},{3,4},{4,5},{5,6},{6,7},{7,0},{8,9},{9,10},{10,1... | collective-permute-start | bytes 1572872 | tf_op jit(solution)/shard_map/ppermute | solution.py:14
  350.6 1.6 copy-start.2
where the time goes:
time: 355 us; the launch traced here: 353 us
  matrix products  103 us (29%)
  blocking collectives  81.9 us (23%)
  other arithmetic  66.1 us (19%)
  loops' own time  46 us (13%)
  waiting for transfers between devices  23.6 us (7%)
  starting transfers between devices  20.4 us (6%)
  local copies, waits for them, and re-layouts  11.1 us (3%)
    psum x1, blocking collectives, shards(): factor = upper_factor(lax.psum(local_gram, ('gx', 'gy')))  81.9 us
    dot_general x64, matrix products, row_step(): jnp.dot(upper_row, inverse, precision=lax.Precision.HIGHEST, preferred_el...  50.1 us
    dot_general x64, matrix products, column_step(): jnp.dot(lower, row_now, precision=lax.Precision.HIGHEST, preferred_elemen...  49.5 us
    another operation x1, loops' own time, upper_factor(): lower = lax.fori_loop(0, order, column_step, jnp.zeros_like(gram))  45.6 us
    reduce_sum x64, other arithmetic, row_step(): pivot = jnp.sum(jnp.where(index == row, upper_row, 0.0))  39.3 us
    ppermute x4, starting transfers between devices, extended(): lax.ppermute(head, axis, [((i + 1) % count, i) for i in range(count)])  18.7 us
    ppermute x4, waiting for transfers between devices, extended(): lax.ppermute(head, axis, [((i + 1) % count, i) for i in range(count)])  17.9 us
    sub x1, other arithmetic, shards(): filtered = 2.0 * (applied - 5.5 * first) / 4.5 - orbitals  7.45 us
  transfers between devices with their start and end apart: 8, of which 7 were waited for; matrix products, arithmetic and copies ran while one was open for 2% of the time, Pallas kernels for 0%

commit v1 on v0

--- a/solution.py
+++ b/solution.py
@@ -84,7 +84,7 @@
         jnp.dot(flat, flat.T, precision=lax.Precision.HIGHEST, preferred_element_type=jnp.float32)
         / cells
     )
-    factor = upper_factor(lax.psum(local_gram, ("gx", "gy")))
+    factor = upper_factor(jnp.sum(lax.all_gather(local_gram, ("gx", "gy")), axis=0))
     inverse = upper_inverse(factor)
     solved = jnp.dot(
         inverse.T, flat, precision=lax.Precision.HIGHEST, preferred_element_type=jnp.float32

time: 355 us -> 411 us (1.16)
  waiting for transfers between devices: 23.6 us -> 145 us
  blocking collectives: 81.9 us -> 0 us
  between operations: 0.88 us -> 14.3 us
    all_gather x0 -> x1, waiting for transfers between devices: none -> 121 us  [shards(): lax.all_gather(local_gram, ('gx', 'gy'))]
    psum x1 -> x0, blocking collectives: 81.9 us -> none  [shards(): factor = upper_factor(lax.psum(local_gram, ('gx', 'gy')))]
  transfers between devices with their start and end apart: 8 -> 9, of which waited for: 7 -> 8; matrix products, arithmetic and copies ran while one was open for 2% -> 1% of each run, Pallas kernels for 0% -> 0%
where the time goes in v1:
time: 411 us; the launch traced here: 410 us
  waiting for transfers between devices  145 us (35%)
  matrix products  104 us (25%)
  other arithmetic  70.2 us (17%)
  loops' own time  46.1 us (11%)
  starting transfers between devices  20.6 us (5%)
  between operations  14.3 us (3%)
  local copies, waits for them, and re-layouts  9.71 us (2%)
    all_gather x1, waiting for transfers between devices, shards(): lax.all_gather(local_gram, ('gx', 'gy'))  121 us
    dot_general x64, matrix products, row_step(): jnp.dot(upper_row, inverse, precision=lax.Precision.HIGHEST, preferred_el...  50.1 us
    dot_general x64, matrix products, column_step(): jnp.dot(lower, row_now, precision=lax.Precision.HIGHEST, preferred_elemen...  49.5 us
    another operation x1, loops' own time, upper_factor(): lower = lax.fori_loop(0, order, column_step, jnp.zeros_like(gram))  45.6 us
    reduce_sum x64, other arithmetic, row_step(): pivot = jnp.sum(jnp.where(index == row, upper_row, 0.0))  39.3 us
    ppermute x4, starting transfers between devices, extended(): lax.ppermute(head, axis, [((i + 1) % count, i) for i in range(count)])  18.8 us
    ppermute x4, waiting for transfers between devices, extended(): lax.ppermute(head, axis, [((i + 1) % count, i) for i in range(count)])  18.2 us
  transfers between devices with their start and end apart: 9, of which 8 were waited for; matrix products, arithmetic and copies ran while one was open for 1% of the time, Pallas kernels for 0%

profile of v1, /device:TPU:1, one launch (start us, length us, event | category | flops | bytes accessed | tf_op | source)
XLA Modules:
  0.0 409.6 jit_solution(6983221593491255411)
XLA Ops:
  7.2 1.4 fusion.60
  8.6 3.3 collective-permute-start
  13.5 4.7 %collective-permute-done = f32[64,2,8,128]{3,2,1,0:T(8,128)S(1)} collective-permute-done((f32[64,2,8,128]{3,2,1,0:T(8,128)S(1)}, f32[64,2,8,128]{3,2,1,0:T(8,128)S(1)}, u32[]{:S(2)}, u32[]{:S(2)}) %collective-permute-start) | collective-permute-done | bytes 524320 | tf_op jit(solution)/shard_map/ppermute | solution.py:16
  19.1 5.7 %collective-permute-start.2 = (f32[64,8,2,128]{3,1,2,0:T(8,128)S(1)}, f32[64,8,2,128]{3,1,2,0:T(8,128)S(1)}, u32[]{:S(2)}, u32[]{:S(2)}) collective-permute-start(f32[64,8,2,128]{3,1,2,0:T(8,128)S(1)} %get-tuple-element.263), channel_id=1, source_target_pairs={{1,0},{2,1},{3,2},{4,3},{5,4},{6,5},{7,6},{0,7},{9,8},{10,9},{11,1... | collective-permute-start | bytes 1572872 | tf_op jit(solution)/shard_map/ppermute | solution.py:16
  26.1 4.8 %collective-permute-done.2 = f32[64,8,2,128]{3,1,2,0:T(8,128)S(1)} collective-permute-done((f32[64,8,2,128]{3,1,2,0:T(8,128)S(1)}, f32[64,8,2,128]{3,1,2,0:T(8,128)S(1)}, u32[]{:S(2)}, u32[]{:S(2)}) %collective-permute-start.2) | collective-permute-done | bytes 524320 | tf_op jit(solution)/shard_map/ppermute | solution.py:16
  30.9 3.1 collective-permute-done.3
  34.0 7.4 %broadcast_multiply_fusion = (f32[64,4,8,128]{3,1,2,0:T(4,128)S(1)}, f32[64,4,8,128]{3,1,2,0:T(4,128)S(1)}) fusion(f32[64,4,8,128]{3,1,2,0:T(4,128)S(1)} %copy.54, f32[4,8,128]{2,0,1:T(4,128)S(1)} %copy.70, f32[64,4,8,2]{3,1,2,0:T(4,128)S(1)} %get-tuple-element.282, f32[64,4,8,126]{3,1,2,0:T(4,128)S(1)} %get-tuple-element.284, ...), kind=kLoop, calls=%fused_computation.105 | loop fusion | flops 11796480 | bytes 9453568 | tf_op jit(solution)/shard_map/div | solution.py:77
  41.9 9.7 %collective-permute-start.4 = (f32[64,2,8,128]{3,2,1,0:T(8,128)S(1)}, f32[64,2,8,128]{3,2,1,0:T(8,128)S(1)}, u32[]{:S(2)}, u32[]{:S(2)}) collective-permute-start(f32[64,2,8,128]{3,2,1,0:T(8,128)S(1)} %copy.73), channel_id=1, source_target_pairs={{8,0},{16,8},{24,16},{32,24},{40,32},{48,40},{56,48},{64,56},{72,6... | collective-permute-start | bytes 1572872 | tf_op jit(solution)/shard_map/ppermute | solution.py:16
  53.2 3.4 collective-permute-done.4
  56.9 1.2 collective-permute-done.5
  58.8 1.5 collective-permute-start.7
  61.5 5.3 %collective-permute-done.6 = f32[64,8,2,128]{3,1,2,0:T(8,128)S(1)} collective-permute-done((f32[64,8,2,128]{3,1,2,0:T(8,128)S(1)}, f32[64,8,2,128]{3,1,2,0:T(8,128)S(1)}, u32[]{:S(2)}, u32[]{:S(2)}) %collective-permute-start.6) | collective-permute-done | bytes 524320 | tf_op jit(solution)/shard_map/ppermute | solution.py:16
  66.8 1.3 collective-permute-done.7
  68.1 7.5 %multiply_subtract_fusion = f32[64,4,8,128]{3,1,2,0:T(4,128)S(1)} fusion(f32[64,4,8,128]{3,1,2,0:T(4,128)S(1)} %get-tuple-element.258, f32[64,4,8,2]{3,1,2,0:T(4,128)S(1)} %get-tuple-element.272, f32[64,4,8,126]{3,1,2,0:T(4,128)S(1)} %get-tuple-element.274, f32[64,4,8,126]{3,1,2,0:T(4,128)S(1)} %get-tuple-element.273, ...), kind=kLoop, calls=%fused_computation.97 | loop fusion | flops 12058624 | bytes 10502144 | tf_op jit(solution)/shard_map/sub | solution.py:79
  75.5 2.7 fusion.17
  78.4 121.1 %all-gather.3.cloned.1.call-done = f32[16384,64]{1,0:T(8,128)} async-done(((f32[64,64]{1,0:T(8,128)}), f32[16384,64]{1,0:T(8,128)}) %all-gather.3.cloned.1.call-update) | async-done | bytes 4194320 | tf_op jit(solution)/shard_map/all_gather | solution.py:87
  199.5 4.0 reduce_sum.38
  203.5 101.3 %while.32 = (s32[]{:T(128)}, f32[64,64]{1,0:T(8,128)S(1)}, f32[64,64]{0,1:T(8,128)S(1)}, s32[]{:T(128)}, s32[]{:T(128)}) while((s32[]{:T(128)}, f32[64,64]{1,0:T(8,128)S(1)}, f32[64,64]{0,1:T(8,128)S(1)}, s32[]{:T(128)}, s32[]{:T(128)}) %tuple.93), condition=%wide.region_3.4_spmd.clone.clone, body=%wide.region_1.3_spmd.clone.clone.sunk | while | flops 62082 | bytes 102112 | solution.py:54
  304.9 95.1 %while.31 = (s32[]{:T(128)}, f32[64,64]{1,0:T(8,128)S(1)}, f32[64,64]{1,0:T(8,128)S(1)}, s32[]{:T(128)}, s32[]{:T(128)}, /*index=5*/s32[]{:T(128)}, s32[]{:T(128)}) while((s32[]{:T(128)}, f32[64,64]{1,0:T(8,128)S(1)}, f32[64,64]{1,0:T(8,128)S(1)}, s32[]{:T(128)}, s32[]{:T(128)}, /*index=5*/s32[]{:T(128)}, s32[]{:T(128)}) %tuple.101), condition=%wide.region_6.7_spmd.clone, body=%wide.region_4.6_spmd.clone.sunk | while | flops 61958 | bytes 67106 | solution.py:73
  307.0 0.8 fusion.75
  308.5 0.8 fusion.75
  310.0 0.8 fusion.75
  311.5 0.8 fusion.75
  313.0 0.8 fusion.75
  315.9 0.8 fusion.75
  317.4 0.8 fusion.75
  318.9 0.8 fusion.75
  320.4 0.8 fusion.75
  321.9 0.8 fusion.75
  323.4 0.8 fusion.75
  400.0 1.6 fusion.16
  401.6 1.2 copy.88
  (604 shorter events, 150.0 us)
Async XLA Ops:
  7.2 4.8 %copy-start = (f32[64,4,8,128]{3,2,1,0:T(8,128)S(1)}, f32[64,4,8,128]{3,2,1,0:T(8,128)}, u32[]{:S(2)}) copy-start(f32[64,4,8,128]{3,2,1,0:T(8,128)} %param.6) | copy-start | bytes 3145732
  7.2 5.0 %copy-start.1 = (f32[4,8,128]{2,1,0:T(8,128)S(1)}, f32[4,8,128]{2,1,0:T(8,128)}, u32[]{:S(2)}) copy-start(f32[4,8,128]{2,1,0:T(8,128)} %param.7) | copy-start | bytes 49156
  7.2 192.3 %all-gather.3.cloned.1.call-start = ((), (), s32[]{:S(2)}) async-start(), calls=%async_computation | async-start | bytes 8421376 | tf_op jit(solution)/shard_map/all_gather | solution.py:87
  8.6 9.6 %collective-permute-start = (f32[64,2,8,128]{3,2,1,0:T(8,128)S(1)}, f32[64,2,8,128]{3,2,1,0:T(8,128)S(1)}, u32[]{:S(2)}, u32[]{:S(2)}) collective-permute-start(f32[64,2,8,128]{3,2,1,0:T(8,128)S(1)} %get-tuple-element.276), channel_id=1, source_target_pairs={{8,0},{16,8},{24,16},{32,24},{40,32},{48,40},{56,48},{64,56},{72,6... | collective-permute-start | bytes 1572872 | tf_op jit(solution)/shard_map/ppermute | solution.py:16
  11.9 6.6 %collective-permute-start.1 = (f32[64,2,8,128]{3,2,1,0:T(8,128)S(1)}, f32[64,2,8,128]{3,2,1,0:T(8,128)S(1)}, u32[]{:S(2)}, u32[]{:S(2)}) collective-permute-start(f32[64,2,8,128]{3,2,1,0:T(8,128)S(1)} %get-tuple-element.275), channel_id=1, source_target_pairs={{0,8},{8,16},{16,24},{24,32},{32,40},{40,48},{48,56},{56,64},{64,7... | collective-permute-start | bytes 1572872 | tf_op jit(solution)/shard_map/ppermute | solution.py:14
  19.1 11.8 %collective-permute-start.2 = (f32[64,8,2,128]{3,1,2,0:T(8,128)S(1)}, f32[64,8,2,128]{3,1,2,0:T(8,128)S(1)}, u32[]{:S(2)}, u32[]{:S(2)}) collective-permute-start(f32[64,8,2,128]{3,1,2,0:T(8,128)S(1)} %get-tuple-element.263), channel_id=1, source_target_pairs={{1,0},{2,1},{3,2},{4,3},{5,4},{6,5},{7,6},{0,7},{9,8},{10,9},{11,1... | collective-permute-start | bytes 1572872 | tf_op jit(solution)/shard_map/ppermute | solution.py:16
  24.8 9.2 %collective-permute-start.3 = (f32[64,8,2,128]{3,1,2,0:T(8,128)S(1)}, f32[64,8,2,128]{3,1,2,0:T(8,128)S(1)}, u32[]{:S(2)}, u32[]{:S(2)}) collective-permute-start(f32[64,8,2,128]{3,1,2,0:T(8,128)S(1)} %get-tuple-element.264), channel_id=1, source_target_pairs={{0,1},{1,2},{2,3},{3,4},{4,5},{5,6},{6,7},{7,0},{8,9},{9,10},{10,1... | collective-permute-start | bytes 1572872 | tf_op jit(solution)/shard_map/ppermute | solution.py:14
  41.9 14.7 %collective-permute-start.4 = (f32[64,2,8,128]{3,2,1,0:T(8,128)S(1)}, f32[64,2,8,128]{3,2,1,0:T(8,128)S(1)}, u32[]{:S(2)}, u32[]{:S(2)}) collective-permute-start(f32[64,2,8,128]{3,2,1,0:T(8,128)S(1)} %copy.73), channel_id=1, source_target_pairs={{8,0},{16,8},{24,16},{32,24},{40,32},{48,40},{56,48},{64,56},{72,6... | collective-permute-start | bytes 1572872 | tf_op jit(solution)/shard_map/ppermute | solution.py:16
  51.7 6.4 %collective-permute-start.5 = (f32[64,2,8,128]{3,2,1,0:T(8,128)S(1)}, f32[64,2,8,128]{3,2,1,0:T(8,128)S(1)}, u32[]{:S(2)}, u32[]{:S(2)}) collective-permute-start(f32[64,2,8,128]{3,2,1,0:T(8,128)S(1)} %copy.75), channel_id=1, source_target_pairs={{0,8},{8,16},{16,24},{24,32},{32,40},{40,48},{48,56},{56,64},{64,7... | collective-permute-start | bytes 1572872 | tf_op jit(solution)/shard_map/ppermute | solution.py:14
  58.7 8.1 %collective-permute-start.6 = (f32[64,8,2,128]{3,1,2,0:T(8,128)S(1)}, f32[64,8,2,128]{3,1,2,0:T(8,128)S(1)}, u32[]{:S(2)}, u32[]{:S(2)}) collective-permute-start(f32[64,8,2,128]{3,1,2,0:T(8,128)S(1)} %get-tuple-element.261), channel_id=1, source_target_pairs={{1,0},{2,1},{3,2},{4,3},{5,4},{6,5},{7,6},{0,7},{9,8},{10,9},{11,1... | collective-permute-start | bytes 1572872 | tf_op jit(solution)/shard_map/ppermute | solution.py:16
  58.8 9.3 %collective-permute-start.7 = (f32[64,8,2,128]{3,1,2,0:T(8,128)S(1)}, f32[64,8,2,128]{3,1,2,0:T(8,128)S(1)}, u32[]{:S(2)}, u32[]{:S(2)}) collective-permute-start(f32[64,8,2,128]{3,1,2,0:T(8,128)S(1)} %get-tuple-element.262), channel_id=1, source_target_pairs={{0,1},{1,2},{2,3},{3,4},{4,5},{5,6},{6,7},{7,0},{8,9},{9,10},{10,1... | collective-permute-start | bytes 1572872 | tf_op jit(solution)/shard_map/ppermute | solution.py:14
  400.0 2.8 copy-start.2
Sparse Core Ops, SparseCore 0:
  78.4 120.9 all-gather.2
